TPU v7x, 32 devices: a whole 2x2x4 slice. The times are simulated.
32 devices in a mesh: seq: 8 (over z, y), fsdp: 4 (over x, core).
Axes of the slice: x: 2, y: 2, z: 4, core: 2. Of those that a mesh axis runs over, the one named last changes fastest.
Arguments:
- tokens: bfloat16 [2048, 2048], P('seq', 'fsdp'), may hold values from -6 to 6
- deal_order: int32 [8, 8], replicated, may hold values from 0 to 7, each once within a row
- lengths: int32 [4], replicated, may hold values from 1 to 1024, 2048 in all
- x_weight: bfloat16 [2048, 1536], P(None, 'fsdp'), may hold values from -0.0390625 to 0.0390625
- z_weight: bfloat16 [2048, 1536], P(None, 'fsdp'), may hold values from -0.125 to 0.125
- shared_weight: bfloat16 [2048, 512], P('fsdp'), may hold values from -0.0390625 to 0.0390625
- step_weight: bfloat16 [2048, 24], P(None, 'fsdp'), may hold values from -0.125 to 0.125
- conv_heads: float32 [4, 1536], P(None, 'fsdp'), may hold values from -3 to 3
- conv_shared: float32 [4, 512], replicated, may hold values from -3 to 3
- step_bias: float32 [24], P('fsdp'), as said below
- decay_log: float32 [24], P('fsdp'), may hold values from -7.1 to -2.8, as said below
- skip_gain: float32 [24], P('fsdp'), may hold values from 0.5 to 1.5
Outputs:
- mixed: bfloat16 [2048, 1536], P('seq', 'fsdp')
Inputs may be any that keep to these rules, and one draw needn't show every extreme that they name: `deal_order`: each row is a permutation of 0 to 7. The lengths sum to 2048. `decay_log`: one value a head. `step_bias`: one value a head.
All inputs are finite; a program needn't handle non-finite values.
Results may differ from a plain program's by a relative error of at most 0.0095.
Values may be sent and summed in bfloat16 or wider, within the bound.
No kernel may reach another device: no remote copies, remote signals or barrier semaphores. Data moves between devices by JAX's collectives and lax.ppermute only.
A program may use at most 128 MiB of HBM per device.

v0:
```python
import jax
import jax.numpy as jnp
from jax import lax
from jax.sharding import PartitionSpec as P

precise = lax.Precision.HIGHEST


def shifted(array, axis, by):
    count = lax.axis_size(axis)
    pairs = [(i, i + by) for i in range(count) if 0 <= i + by < count]
    return lax.ppermute(array, axis, pairs)


def combine_packed(earlier, later):
    rows = later.shape[1] - 1
    d_e, d_l = (earlier[:, rows:, :], later[:, rows:, :])
    return jnp.concatenate([d_l * earlier[:, :rows, :] + later[:, :rows, :], d_e * d_l], axis=1)


def received(packed, axis, by):
    place = lax.axis_index(axis)
    got = shifted(packed, axis, by)
    rows = packed.shape[1] - 1
    missing = (place < by).astype(packed.dtype)
    return got.at[:, rows:, :].add(missing)


def exclusive_scan(packed, axis):
    count = lax.axis_size(axis)
    if count == 1:
        return received(packed, axis, 1)
    held = received(packed, axis, 1)
    if count > 2:
        held = combine_packed(received(packed, axis, 2), held)
    cover = 2
    while cover < count - 1:
        held = combine_packed(received(held, axis, cover), held)
        cover *= 2
    return held


def segment_of(positions, lengths):
    prompt_ends = jnp.cumsum(lengths)
    counted = (positions[:, None] >= prompt_ends[None, :]).astype(jnp.int32)
    return jnp.sum(counted, axis=1)


def causal_conv(extended, segment_ids, weights, conv_width):
    out_rows = extended.shape[0] - conv_width + 1
    target = segment_ids[conv_width - 1 :]
    running = jnp.zeros((out_rows, extended.shape[1]), jnp.float32)
    for tap_index in range(conv_width):
        matched = (segment_ids[tap_index : tap_index + out_rows] == target).astype(jnp.float32)
        running = (
            running
            + weights[tap_index][None, :]
            * extended[tap_index : tap_index + out_rows]
            * matched[:, None]
        )
    return running


def local_terms(x_heads, b_rows, c_rows, step_size, decay_log, segment_ids, seg_before):
    log_decay = -jnp.exp(decay_log)[None, :] * step_size
    cum_decay = jnp.cumsum(log_decay, axis=0)
    positions_in = jnp.arange(x_heads.shape[0], dtype=jnp.int32)
    same_prompt = (segment_ids[:, None] == segment_ids[None, :]) & (
        positions_in[:, None] >= positions_in[None, :]
    )
    decay_gap = cum_decay.T[:, :, None] - cum_decay.T[:, None, :]
    decay_matrix = jnp.exp(jnp.where(same_prompt[None], decay_gap, -jnp.inf))
    scores = jnp.dot(c_rows, b_rows.T, precision=precise)
    x_step = x_heads * step_size[:, :, None]
    intra = jnp.einsum("hts,shp->thp", scores[None] * decay_matrix, x_step, precision=precise)
    to_end = jnp.exp(
        jnp.where(
            (segment_ids == segment_ids[-1])[:, None], cum_decay[-1][None, :] - cum_decay, -jnp.inf
        )
    )
    state_out = jnp.einsum("shp,sn->hpn", x_step * to_end[:, :, None], b_rows, precision=precise)
    carried = segment_ids == seg_before
    carry_in = jnp.exp(jnp.where(carried[:, None], cum_decay, -jnp.inf))
    block_decay = jnp.where(carried[-1], jnp.exp(cum_decay[-1]), 0.0)
    return (intra, state_out, carry_in, block_decay)


def per_device(
    tokens,
    deal_order,
    lengths,
    x_weight,
    z_weight,
    shared_weight,
    step_weight,
    conv_heads,
    conv_shared,
    step_bias,
    decay_log,
    skip_gain,
):
    seq_count = lax.axis_size("seq")
    own_index = lax.axis_index("seq")
    tok_dev = tokens.shape[0]
    piece_rows = tok_dev // seq_count
    slot_rows = tokens.reshape(seq_count, piece_rows, tokens.shape[1])
    arrived = lax.all_to_all(slot_rows, "seq", split_axis=0, concat_axis=0, tiled=True)
    dealt_row = lax.dynamic_slice_in_dim(deal_order, own_index, 1, 0)[0]
    inverse = jnp.argsort(dealt_row)
    stream_block = jnp.take(arrived, inverse, axis=0).reshape(tok_dev, tokens.shape[1])
    inner_dev = x_weight.shape[1]
    heads_dev = step_weight.shape[1]
    head_dim = inner_dev // heads_dev
    state_dim = shared_weight.shape[1] // 2
    w_full = lax.all_gather(shared_weight, "fsdp", axis=0, tiled=True)
    weight_list = (x_weight, z_weight, step_weight, w_full)
    feature_part = lax.all_gather(stream_block, "fsdp", axis=1, tiled=True)
    x_acc, z_acc, step_acc, bc_acc = tuple(
        (
            jnp.dot(feature_part, weight, preferred_element_type=jnp.float32)
            for weight in weight_list
        )
    )
    x_raw = x_acc.astype(jnp.bfloat16)
    z_raw = z_acc.astype(jnp.bfloat16)
    bc_raw = bc_acc.astype(jnp.bfloat16)
    step_size = jax.nn.softplus(step_acc + step_bias[None, :])
    mixed_in = jnp.concatenate([x_raw, bc_raw], axis=1)
    conv_width = conv_heads.shape[0]
    prior_rows = shifted(mixed_in[tok_dev - conv_width + 1 :], "seq", 1)
    first_pos = own_index * tok_dev
    positions = first_pos - (conv_width - 1) + jnp.arange(tok_dev + conv_width - 1, dtype=jnp.int32)
    seg_ext = segment_of(positions, lengths)
    extended = jnp.concatenate([prior_rows, mixed_in], axis=0).astype(jnp.float32)
    activated = jax.nn.silu(
        causal_conv(
            extended, seg_ext, jnp.concatenate([conv_heads, conv_shared], axis=1), conv_width
        )
    )
    segment_ids = seg_ext[conv_width - 1 :]
    seg_before = jnp.where(own_index == 0, -1, seg_ext[conv_width - 2])
    x_heads = activated[:, :inner_dev].reshape(tok_dev, heads_dev, head_dim)
    b_rows = activated[:, inner_dev : inner_dev + state_dim]
    c_rows = activated[:, inner_dev + state_dim :]
    intra, state_out, carry_in, block_decay = local_terms(
        x_heads, b_rows, c_rows, step_size, decay_log, segment_ids, seg_before
    )
    packed = jnp.concatenate(
        [state_out, jnp.broadcast_to(block_decay[:, None, None], (heads_dev, 1, state_dim))], axis=1
    )
    state_in = exclusive_scan(packed, "seq")[:, :head_dim, :]
    incoming = jnp.einsum("tn,hpn->thp", c_rows, state_in, precision=precise)
    y_block = intra + carry_in[:, :, None] * incoming + skip_gain[None, :, None] * x_heads
    gated = (y_block.reshape(tok_dev, inner_dev) * jax.nn.silu(z_raw.astype(jnp.float32))).astype(
        jnp.bfloat16
    )
    ordered = gated.reshape(seq_count, piece_rows, inner_dev)
    outgoing = jnp.take(ordered, dealt_row, axis=0)
    returned = lax.all_to_all(outgoing, "seq", split_axis=0, concat_axis=0, tiled=True)
    return returned.reshape(tok_dev, inner_dev)


def solution(mesh):
    return jax.shard_map(
        per_device,
        mesh=mesh,
        in_specs=(
            P("seq", "fsdp"),
            P(),
            P(),
            P(None, "fsdp"),
            P(None, "fsdp"),
            P("fsdp", None),
            P(None, "fsdp"),
            P(None, "fsdp"),
            P(),
            P("fsdp"),
            P("fsdp"),
            P("fsdp"),
        ),
        out_specs=P("seq", "fsdp"),
        check_vma=False,
    )
```

profile of v0, /device:TPU:0, one launch (start us, length us, event | category | flops | bytes accessed | tf_op | source)
XLA Modules:
  0.0 161.2 jit_solution(1924981026122222076)
XLA Ops:
  6.6 7.4 %all-to-all-start = ((bf16[8,32,512]{2,1,0:T(8,128)(2,1)}), bf16[8,32,512]{2,1,0:T(8,128)(2,1)S(1)}, u32[]{:S(2)}, u32[]{:S(2)}) async-start(bf16[8,32,512]{2,1,0:T(8,128)(2,1)} %bitcast.85), calls=%async_computation | async-start | bytes 524288 | tf_op jit(solution)/shard_map/all_to_all | solution.py:107
  14.0 1.3 compare_and_fusion.1
  15.3 1.0 sort.17
  16.5 6.4 %all-to-all-done = bf16[8,32,512]{2,1,0:T(8,128)(2,1)S(1)} async-done(((bf16[8,32,512]{2,1,0:T(8,128)(2,1)}), bf16[8,32,512]{2,1,0:T(8,128)(2,1)S(1)}, u32[]{:S(2)}, u32[]{:S(2)}) %all-to-all-start) | async-done | bytes 262176 | tf_op jit(solution)/shard_map/all_to_all | solution.py:107
  22.9 0.6 gather_fusion
  23.5 0.8 bitcast_select_fusion
  24.4 0.7 all-gather.5.cloned.1.call-update
  25.4 0.6 fusion.53
  26.5 1.3 broadcast_compare_fusion
  27.9 0.7 slice.199
  28.5 0.6 slice_reduce_fusion.4
  29.2 11.1 %all-gather.3.cloned.1.call-done = bf16[256,2048]{1,0:T(8,128)(2,1)} async-done(((bf16[256,512]{1,0:T(8,128)(2,1)}), bf16[256,2048]{1,0:T(8,128)(2,1)}) %all-gather.3.cloned.1.call-update) | async-done | bytes 1048592 | tf_op jit(solution)/shard_map/all_gather | solution.py:117
  40.2 1.6 %fusion.41 = (f32[6,256]{1,0:T(8,128)S(1)}, f32[256,6]{0,1:T(8,128)S(1)}) fusion(f32[6]{0:T(128)S(1)} %exponential_negate_fusion, f32[6]{0:T(128)S(1)} %copy-done.19, bf16[256,2048]{1,0:T(8,128)(2,1)} %all-gather.3.cloned.1.call-done, bf16[2048,6]{0,1:T(8,128)(2,1)S(1)} %copy-done.4), kind=kOutput, calls=%fused_computation.64 | convolution fusion | flops 6303744 | bytes 1085488 | tf_op jit(solution)/shard_map/dot_general | solution.py:120
  41.9 1.8 %reduce-window.19 = f32[6,2,128]{2,1,0:T(2,128)S(1)} reduce-window(f32[6,2,128]{2,1,0:T(2,128)S(1)} %reshape.288, f32[]{:T(128)} %constant.149.clone.1), window={size=1x1x128 pad=0_0x0_0x127_0}, to_apply=%region_3.4 | reduce-window | flops 195072 | bytes 12292 | tf_op jit(solution)/shard_map/reduce-window.1
  44.3 0.4 copy-done.7
  44.7 0.7 select_exponential_fusion.1
  45.4 1.9 %convolution_convert_fusion.2 = bf16[256,384]{1,0:T(8,128)(2,1)S(1)} fusion(bf16[256,2048]{1,0:T(8,128)(2,1)} %all-gather.3.cloned.1.call-done, bf16[2048,384]{1,0:T(8,128)(2,1)S(1)} %copy-done), kind=kOutput, calls=%fused_computation.14 | convolution fusion | flops 402751488 | bytes 2818048 | tf_op jit(solution)/shard_map/dot_general | solution.py:120
  47.3 17.1 %all-gather.5.cloned.1.call-done = bf16[2048,512]{1,0:T(8,128)(2,1)} async-done(((bf16[512,512]{1,0:T(8,128)(2,1)}), bf16[2048,512]{1,0:T(8,128)(2,1)}) %all-gather.5.cloned.1.call-update) | async-done | bytes 2097168 | tf_op jit(solution)/shard_map/all_gather | solution.py:115
  64.4 2.3 %convolution_convert_fusion = bf16[256,512]{1,0:T(8,128)(2,1)S(1)} fusion(bf16[256,2048]{1,0:T(8,128)(2,1)S(1)} %copy-done.1, bf16[2048,512]{1,0:T(8,128)(2,1)} %all-gather.5.cloned.1.call-done), kind=kOutput, calls=%fused_computation.8 | convolution fusion | flops 537001984 | bytes 3407872 | tf_op jit(solution)/shard_map/dot_general | solution.py:120
  66.8 3.4 %collective-permute-start = (bf16[3,896]{1,0:T(4,128)(2,1)S(1)}, bf16[3,896]{1,0:T(4,128)(2,1)S(1)}, u32[]{:S(2)}, u32[]{:S(2)}) collective-permute-start(bf16[3,896]{1,0:T(4,128)(2,1)S(1)} %pad_maximum_fusion.3), channel_id=1, source_target_pairs={{0,4},{4,8},{8,12},{12,16},{16,20},{20,24},{24,28},{1,5},{5,9},{9,... | collective-permute-start | bytes 16136 | tf_op jit(solution)/shard_map/ppermute | solution.py:12
  70.2 1.2 broadcast_select_fusion.1
  71.7 0.7 divide_multiply_fusion
  72.4 0.8 slice.219
  73.1 1.9 %copy.39 = f32[256,384]{0,1:T(8,128)} copy(f32[256,384]{1,0:T(8,128)} %slice.219) | data formatting | bytes 786432 | tf_op jit(solution)/shard_map/slice | solution.py:142
  75.1 1.5 fusion.25
  76.5 0.7 broadcast_in_dim.104
  77.3 0.8 pad_maximum_fusion
  78.1 5.9 %collective-permute-start.2 = (f32[6,65,256]{2,1,0:T(8,128)}, f32[6,65,256]{2,1,0:T(8,128)}, u32[]{:S(2)}, u32[]{:S(2)}) collective-permute-start(f32[6,65,256]{2,1,0:T(8,128)} %pad_maximum_fusion), channel_id=1, source_target_pairs={{0,8},{4,12},{8,16},{12,20},{16,24},{20,28},{1,9},{5,13},{9,17},{1... | collective-permute-start | bytes 1198088 | tf_op jit(solution)/shard_map/ppermute | solution.py:12
  83.9 3.2 %collective-permute-start.1 = (f32[6,65,256]{2,1,0:T(8,128)}, f32[6,65,256]{2,1,0:T(8,128)}, u32[]{:S(2)}, u32[]{:S(2)}) collective-permute-start(f32[6,65,256]{2,1,0:T(8,128)} %pad_maximum_fusion), channel_id=1, source_target_pairs={{0,4},{4,8},{8,12},{12,16},{16,20},{20,24},{24,28},{1,5},{5,9},{9,... | collective-permute-start | bytes 1198088 | tf_op jit(solution)/shard_map/ppermute | solution.py:12
  87.2 0.7 slice.182
  87.8 0.8 fusion.49
  88.7 0.9 fusion.31
  89.5 2.6 %collective-permute-done.2 = f32[6,65,256]{2,1,0:T(8,128)} collective-permute-done((f32[6,65,256]{2,1,0:T(8,128)}, f32[6,65,256]{2,1,0:T(8,128)}, u32[]{:S(2)}, u32[]{:S(2)}) %collective-permute-start.2) | collective-permute-done | bytes 399392 | tf_op jit(solution)/shard_map/ppermute | solution.py:12
  92.1 3.0 %collective-permute-done.1 = f32[6,65,256]{2,1,0:T(8,128)} collective-permute-done((f32[6,65,256]{2,1,0:T(8,128)}, f32[6,65,256]{2,1,0:T(8,128)}, u32[]{:S(2)}, u32[]{:S(2)}) %collective-permute-start.1) | collective-permute-done | bytes 399392 | tf_op jit(solution)/shard_map/ppermute | solution.py:12
  95.1 0.8 fusion.47
  96.0 1.2 slice_add_fusion
  97.2 10.9 %collective-permute-start.3 = (f32[6,65,256]{2,1,0:T(8,128)S(1)}, f32[6,65,256]{2,1,0:T(8,128)S(1)}, u32[]{:S(2)}, u32[]{:S(2)}) collective-permute-start(f32[6,65,256]{2,1,0:T(8,128)S(1)} %pad_maximum_fusion.1), channel_id=1, source_target_pairs={{0,8},{4,12},{8,16},{12,20},{16,24},{20,28},{1,9},{5,13},{9,17},{1... | collective-permute-start | bytes 1198088 | tf_op jit(solution)/shard_map/ppermute | solution.py:12
  108.1 0.6 pad_clamp_fusion
  108.7 1.4 fusion.10
  110.2 5.7 %collective-permute-done.3 = f32[6,65,256]{2,1,0:T(8,128)S(1)} collective-permute-done((f32[6,65,256]{2,1,0:T(8,128)S(1)}, f32[6,65,256]{2,1,0:T(8,128)S(1)}, u32[]{:S(2)}, u32[]{:S(2)}) %collective-permute-start.3) | collective-permute-done | bytes 399392 | tf_op jit(solution)/shard_map/ppermute | solution.py:12
  116.0 5.3 %collective-permute-start.4 = (f32[6,65,256]{2,1,0:T(8,128)S(1)}, f32[6,65,256]{2,1,0:T(8,128)S(1)}, u32[]{:S(2)}, u32[]{:S(2)}) collective-permute-start(f32[6,65,256]{2,1,0:T(8,128)S(1)} %pad_maximum_fusion.2), channel_id=1, source_target_pairs={{0,16},{4,20},{8,24},{12,28},{1,17},{5,21},{9,25},{13,29},{2,18},{... | collective-permute-start | bytes 1198088 | tf_op jit(solution)/shard_map/ppermute | solution.py:12
  121.7 1.9 %fusion.5 = f32[256,6,64]{0,2,1:T(8,128)S(1)} fusion(f32[6,256]{1,0:T(8,128)S(1)} %bitcast.90, f32[256,256]{1,0:T(8,128)S(1)} %fusion.33, pred[256,256]{1,0:T(8,128)(4,1)S(1)} %fusion.31, f32[256,6,64]{0,2,1:T(8,128)S(1)} %bitcast.80, f32[256,6]{0,1:T(8,128)S(1)} %get-tuple-element.76), kind=kOutput, calls=%fused_computation.7 | convolution fusion | flops 303267840 | bytes 1126400 | tf_op jit(solution)/shard_map/hts,shp->thp/dot_general | solution.py:75
  123.6 4.5 %collective-permute-done.4 = f32[6,65,256]{2,1,0:T(8,128)S(1)} collective-permute-done((f32[6,65,256]{2,1,0:T(8,128)S(1)}, f32[6,65,256]{2,1,0:T(8,128)S(1)}, u32[]{:S(2)}, u32[]{:S(2)}) %collective-permute-start.4) | collective-permute-done | bytes 399392 | tf_op jit(solution)/shard_map/ppermute | solution.py:12
  128.1 0.5 fusion.9
  128.8 1.1 multiply_convert_fusion
  129.9 0.7 gather_fusion.1
  130.8 22.9 %all_to_all.10 = bf16[8,32,384]{2,1,0:T(8,128)(2,1)S(1)} all-to-all(bf16[8,32,384]{2,1,0:T(8,128)(2,1)S(1)} %broadcast_select_fusion), channel_id=1, replica_groups=mesh['seq'=8,'fsdp'=4] {'seq'}, dimensions={0} | all-to-all | bytes 393216 | tf_op jit(solution)/shard_map/all_to_all | solution.py:159
  153.7 0.7 copy.63
  (82 shorter events, 2.3 us)
Async XLA Ops:
  6.5 38.8 %copy-start = (bf16[2048,384]{1,0:T(8,128)(2,1)S(1)}, bf16[2048,384]{1,0:T(8,128)(2,1)}, u32[]{:S(2)}) copy-start(bf16[2048,384]{1,0:T(8,128)(2,1)} %param.23) | copy-start | bytes 4718596
  6.5 18.5 %copy-start.21 = (s32[4]{0:T(128)S(1)}, s32[4]{0:T(128)}, u32[]{:S(2)}) copy-start(s32[4]{0:T(128)} %param.22) | copy-start | bytes 52
  6.5 22.0 %copy-start.14 = (f32[4,384]{1,0:T(4,128)S(1)}, f32[4,384]{1,0:T(4,128)}, u32[]{:S(2)}) copy-start(f32[4,384]{1,0:T(4,128)} %param.27) | copy-start | bytes 18436
  6.5 22.0 %copy-start.13 = (f32[4,512]{1,0:T(4,128)S(1)}, f32[4,512]{1,0:T(4,128)}, u32[]{:S(2)}) copy-start(f32[4,512]{1,0:T(4,128)} %param.28) | copy-start | bytes 24580
  6.5 22.6 %copy-start.22 = (f32[6]{0:T(128)S(1)}, f32[6]{0:T(128)}, u32[]{:S(2)}) copy-start(f32[6]{0:T(128)} %param.30) | copy-start | bytes 76
  6.5 33.7 %copy-start.19 = (f32[6]{0:T(128)S(1)}, f32[6]{0:T(128)}, u32[]{:S(2)}) copy-start(f32[6]{0:T(128)} %param.29) | copy-start | bytes 76
  6.6 33.7 %copy-start.4 = (bf16[2048,6]{0,1:T(8,128)(2,1)S(1)}, bf16[2048,6]{0,1:T(8,128)(2,1)}, u32[]{:S(2)}) copy-start(bf16[2048,6]{0,1:T(8,128)(2,1)} %param.26) | copy-start | bytes 73732
  6.6 16.3 %all-to-all-start = ((bf16[8,32,512]{2,1,0:T(8,128)(2,1)}), bf16[8,32,512]{2,1,0:T(8,128)(2,1)S(1)}, u32[]{:S(2)}, u32[]{:S(2)}) async-start(bf16[8,32,512]{2,1,0:T(8,128)(2,1)} %bitcast.85), calls=%async_computation | async-start | bytes 524288 | tf_op jit(solution)/shard_map/all_to_all | solution.py:107
  14.0 26.2 %all-gather.3.cloned.1.call-start = ((), (), s32[]{:S(2)}) async-start(), calls=%async_computation.2 | async-start | bytes 1310720 | tf_op jit(solution)/shard_map/all_gather | solution.py:117
  24.3 40.1 %all-gather.5.cloned.1.call-start = ((), (), s32[]{:S(2)}) async-start(), calls=%async_computation.3 | async-start | bytes 2621440 | tf_op jit(solution)/shard_map/all_gather | solution.py:115
  25.4 14.9 %copy-start.5 = (s32[259]{0:T(512)}, s32[259]{0:T(512)S(1)}, u32[]{:S(2)}) copy-start(s32[259]{0:T(512)S(1)} %convert_reduce_fusion) | copy-start | bytes 3112
  41.9 22.5 %copy-start.1 = (bf16[256,2048]{1,0:T(8,128)(2,1)S(1)}, bf16[256,2048]{1,0:T(8,128)(2,1)}, u32[]{:S(2)}) copy-start(bf16[256,2048]{1,0:T(8,128)(2,1)} %all-gather.3.cloned.1.call-done) | copy-start | bytes 3145732
  44.1 0.6 copy-start.7
  66.7 4.9 %copy-start.9 = (f32[896]{0:T(1024)S(1)}, f32[896]{0:T(1024)}, u32[]{:S(2)}) copy-start(f32[896]{0:T(1024)} %get-tuple-element.55) | copy-start | bytes 10756
  66.7 4.9 %copy-start.10 = (f32[896]{0:T(1024)S(1)}, f32[896]{0:T(1024)}, u32[]{:S(2)}) copy-start(f32[896]{0:T(1024)} %get-tuple-element.56) | copy-start | bytes 10756
  66.7 4.9 %copy-start.11 = (f32[896]{0:T(1024)S(1)}, f32[896]{0:T(1024)}, u32[]{:S(2)}) copy-start(f32[896]{0:T(1024)} %get-tuple-element.57) | copy-start | bytes 10756
  66.7 4.9 %copy-start.12 = (f32[896]{0:T(1024)S(1)}, f32[896]{0:T(1024)}, u32[]{:S(2)}) copy-start(f32[896]{0:T(1024)} %get-tuple-element.58) | copy-start | bytes 10756
  66.7 4.9 %copy-start.15 = (f32[256]{0:T(256)S(1)}, f32[256]{0:T(256)}, u32[]{:S(2)}) copy-start(f32[256]{0:T(256)} %get-tuple-element.69) | copy-start | bytes 3076
  66.8 4.9 %copy-start.16 = (f32[256]{0:T(256)S(1)}, f32[256]{0:T(256)}, u32[]{:S(2)}) copy-start(f32[256]{0:T(256)} %get-tuple-element.70) | copy-start | bytes 3076
  66.8 4.9 %copy-start.17 = (f32[256]{0:T(256)S(1)}, f32[256]{0:T(256)}, u32[]{:S(2)}) copy-start(f32[256]{0:T(256)} %get-tuple-element.71) | copy-start | bytes 3076
  66.8 4.7 %collective-permute-start = (bf16[3,896]{1,0:T(4,128)(2,1)S(1)}, bf16[3,896]{1,0:T(4,128)(2,1)S(1)}, u32[]{:S(2)}, u32[]{:S(2)}) collective-permute-start(bf16[3,896]{1,0:T(4,128)(2,1)S(1)} %pad_maximum_fusion.3), channel_id=1, source_target_pairs={{0,4},{4,8},{8,12},{12,16},{16,20},{20,24},{24,28},{1,5},{5,9},{9,... | collective-permute-start | bytes 16136 | tf_op jit(solution)/shard_map/ppermute | solution.py:12
  75.0 12.1 %copy-start.6 = (s32[259]{0:T(512)S(1)}, s32[259]{0:T(512)}, u32[]{:S(2)}) copy-start(s32[259]{0:T(512)} %copy-done.5) | copy-start | bytes 3112
  78.1 14.1 %collective-permute-start.2 = (f32[6,65,256]{2,1,0:T(8,128)}, f32[6,65,256]{2,1,0:T(8,128)}, u32[]{:S(2)}, u32[]{:S(2)}) collective-permute-start(f32[6,65,256]{2,1,0:T(8,128)} %pad_maximum_fusion), channel_id=1, source_target_pairs={{0,8},{4,12},{8,16},{12,20},{16,24},{20,28},{1,9},{5,13},{9,17},{1... | collective-permute-start | bytes 1198088 | tf_op jit(solution)/shard_map/ppermute | solution.py:12
  83.9 11.2 %collective-permute-start.1 = (f32[6,65,256]{2,1,0:T(8,128)}, f32[6,65,256]{2,1,0:T(8,128)}, u32[]{:S(2)}, u32[]{:S(2)}) collective-permute-start(f32[6,65,256]{2,1,0:T(8,128)} %pad_maximum_fusion), channel_id=1, source_target_pairs={{0,4},{4,8},{8,12},{12,16},{16,20},{20,24},{24,28},{1,5},{5,9},{9,... | collective-permute-start | bytes 1198088 | tf_op jit(solution)/shard_map/ppermute | solution.py:12
  87.8 20.9 %copy-start.3 = (bf16[2048,384]{1,0:T(8,128)(2,1)S(1)}, bf16[2048,384]{1,0:T(8,128)(2,1)}, u32[]{:S(2)}) copy-start(bf16[2048,384]{1,0:T(8,128)(2,1)} %param.24) | copy-start | bytes 4718596
  97.2 18.7 %collective-permute-start.3 = (f32[6,65,256]{2,1,0:T(8,128)S(1)}, f32[6,65,256]{2,1,0:T(8,128)S(1)}, u32[]{:S(2)}, u32[]{:S(2)}) collective-permute-start(f32[6,65,256]{2,1,0:T(8,128)S(1)} %pad_maximum_fusion.1), channel_id=1, source_target_pairs={{0,8},{4,12},{8,16},{12,20},{16,24},{20,28},{1,9},{5,13},{9,17},{1... | collective-permute-start | bytes 1198088 | tf_op jit(solution)/shard_map/ppermute | solution.py:12
  110.2 11.6 %copy-start.2 = (f32[256,384]{0,1:T(8,128)S(1)}, f32[256,384]{0,1:T(8,128)}, u32[]{:S(2)}) copy-start(f32[256,384]{0,1:T(8,128)} %copy.39) | copy-start | bytes 1179652
  110.2 11.6 %copy-start.8 = (f32[1,6,2,128]{3,1,2,0:T(8,128)S(1)}, f32[1,6,2,128]{3,1,2,0:T(8,128)}, u32[]{:S(2)}) copy-start(f32[1,6,2,128]{3,1,2,0:T(8,128)} %copy-done.7) | copy-start | bytes 18436
  115.9 12.2 %copy-start.20 = (f32[6]{0:T(128)S(1)}, f32[6]{0:T(128)}, u32[]{:S(2)}) copy-start(f32[6]{0:T(128)} %param.31) | copy-start | bytes 76
  116.0 12.2 %collective-permute-start.4 = (f32[6,65,256]{2,1,0:T(8,128)S(1)}, f32[6,65,256]{2,1,0:T(8,128)S(1)}, u32[]{:S(2)}, u32[]{:S(2)}) collective-permute-start(f32[6,65,256]{2,1,0:T(8,128)S(1)} %pad_maximum_fusion.2), channel_id=1, source_target_pairs={{0,16},{4,20},{8,24},{12,28},{1,17},{5,21},{9,25},{13,29},{2,18},{... | collective-permute-start | bytes 1198088 | tf_op jit(solution)/shard_map/ppermute | solution.py:12
  128.7 2.0 %copy-start.18 = (pred[8]{0:T(512)(128)(4,1)S(1)}, pred[8]{0:T(512)(128)(4,1)}, u32[]{:S(2)}) copy-start(pred[8]{0:T(512)(128)(4,1)} %get-tuple-element.59) | copy-start | bytes 28
Sparse Core Ops, SparseCore 0:
  24.4 15.7 all-gather.2
  41.8 22.5 all-gather.4
where the time goes:
time: 162 us; the launch traced here: 161 us
  waiting for transfers between devices  51.2 us (32%)
  starting transfers between devices  36.3 us (22%)
  blocking collectives  22.9 us (14%)
  other arithmetic  15.7 us (10%)
  between operations  14.4 us (9%)
  matrix products  11.6 us (7%)
  local copies, waits for them, and re-layouts  9.22 us (6%)
    ppermute x5, starting transfers between devices, shifted(): return lax.ppermute(array, axis, pairs)  28.8 us
    all_to_all x1, blocking collectives, per_device(): lax.all_to_all(outgoing, 'seq', split_axis=0, concat_axis=0, tiled=True)  22.9 us
    all_gather x1, waiting for transfers between devices, per_device(): w_full = lax.all_gather(shared_weight, 'fsdp', axis=0, tiled=True)  17.1 us
    ppermute x5, waiting for transfers between devices, shifted(): return lax.ppermute(array, axis, pairs)  15.9 us
    all_gather x1, waiting for transfers between devices, per_device(): feature_part = lax.all_gather(stream_block, 'fsdp', axis=1, tiled=True)  11.1 us
    all_to_all x1, starting transfers between devices, per_device(): lax.all_to_all(slot_rows, 'seq', split_axis=0, concat_axis=0, tiled=True)  7.42 us
    dot_general x4, matrix products, per_device(): jnp.dot(feature_part, weight, preferred_element_type=jnp.float32)  7.29 us
    all_to_all x1, waiting for transfers between devices, per_device(): lax.all_to_all(slot_rows, 'seq', split_axis=0, concat_axis=0, tiled=True)  6.42 us
  transfers between devices with their start and end apart: 8, of which 8 were waited for; matrix products, arithmetic and copies ran while one was open for 13% of the time, Pallas kernels for 0%

commit v1 on v0

--- a/solution.py
+++ b/solution.py
@@ -114,7 +114,14 @@
     state_dim = shared_weight.shape[1] // 2
     w_full = lax.all_gather(shared_weight, "fsdp", axis=0, tiled=True)
     weight_list = (x_weight, z_weight, step_weight, w_full)
-    feature_part = lax.all_gather(stream_block, "fsdp", axis=1, tiled=True)
+    ways, here = (lax.axis_size("fsdp"), lax.axis_index("fsdp"))
+    feature_part, reach = (stream_block, 1)
+    while reach < ways:
+        theirs = lax.ppermute(feature_part, "fsdp", [(d, d ^ reach) for d in range(ways)])
+        mine_first = jnp.concatenate([feature_part, theirs], axis=1)
+        theirs_first = jnp.concatenate([theirs, feature_part], axis=1)
+        feature_part = jnp.where(here & reach == 0, mine_first, theirs_first)
+        reach = 2 * reach
     x_acc, z_acc, step_acc, bc_acc = tuple(
         (
             jnp.dot(feature_part, weight, preferred_element_type=jnp.float32)

time: 162 us -> 140 us (0.86)
  waiting for transfers between devices: 51.2 us -> 39.7 us
  local copies, waits for them, and re-layouts: 9.22 us -> 4.26 us
  other arithmetic: 15.7 us -> 12.1 us
  matrix products: 11.6 us -> 8.26 us
    all_gather x1, waiting for transfers between devices: 17.1 us -> 0.02 us  [per_device(): w_full = lax.all_gather(shared_weight, 'fsdp', axis=0, tiled=True)]
    ppermute x0 -> x2, waiting for transfers between devices: none -> 15.4 us  [per_device(): lax.ppermute(feature_part, 'fsdp', [(d, d ^ reach) for d in range(ways)])]
    all_gather x1 -> x0, waiting for transfers between devices: 11.1 us -> none  [per_device(): feature_part = lax.all_gather(stream_block, 'fsdp', axis=1, tiled=True)]
    slice x2, local copies, waits for them, and re-layouts: 2.68 us -> 0.19 us  [per_device(): x_heads = activated[:, :inner_dev].reshape(tok_dev, heads_dev, head_dim)]
    dot_general x4, matrix products: 7.29 us -> 4.95 us  [per_device(): jnp.dot(feature_part, weight, preferred_element_type=jnp.float32)]
    ppermute x0 -> x2, starting transfers between devices: none -> 1.63 us  [per_device(): lax.ppermute(feature_part, 'fsdp', [(d, d ^ reach) for d in range(ways)])]
  transfers between devices with their start and end apart: 8 -> 9, of which waited for: 8 -> 7; matrix products, arithmetic and copies ran while one was open for 13% -> 10% of each run, Pallas kernels for 0% -> 0%
where the time goes in v1:
time: 140 us; the launch traced here: 139 us
  waiting for transfers between devices  39.7 us (28%)
  starting transfers between devices  37.7 us (27%)
  blocking collectives  22.9 us (16%)
  between operations  14.4 us (10%)
  other arithmetic  12.1 us (9%)
  matrix products  8.26 us (6%)
  local copies, waits for them, and re-layouts  4.26 us (3%)
    ppermute x5, starting transfers between devices, shifted(): return lax.ppermute(array, axis, pairs)  28.7 us
    all_to_all x1, blocking collectives, per_device(): lax.all_to_all(outgoing, 'seq', split_axis=0, concat_axis=0, tiled=True)  22.9 us
    ppermute x5, waiting for transfers between devices, shifted(): return lax.ppermute(array, axis, pairs)  17.5 us
    ppermute x2, waiting for transfers between devices, per_device(): lax.ppermute(feature_part, 'fsdp', [(d, d ^ reach) for d in range(ways)])  15.4 us
    all_to_all x1, starting transfers between devices, per_device(): lax.all_to_all(slot_rows, 'seq', split_axis=0, concat_axis=0, tiled=True)  7.29 us
    all_to_all x1, waiting for transfers between devices, per_device(): lax.all_to_all(slot_rows, 'seq', split_axis=0, concat_axis=0, tiled=True)  6.15 us
    dot_general x4, matrix products, per_device(): jnp.dot(feature_part, weight, preferred_element_type=jnp.float32)  4.95 us
  transfers between devices with their start and end apart: 9, of which 7 were waited for; matrix products, arithmetic and copies ran while one was open for 10% of the time, Pallas kernels for 0%

profile of v1, /device:TPU:0, one launch (start us, length us, event | category | flops | bytes accessed | tf_op | source)
XLA Modules:
  0.0 139.4 jit_solution(15358585351118157686)
XLA Ops:
  6.6 0.7 all-gather.2.cloned.1.call-update
  7.3 7.3 %all-to-all-start = ((bf16[8,32,512]{2,1,0:T(8,128)(2,1)}), bf16[8,32,512]{2,1,0:T(8,128)(2,1)S(1)}, u32[]{:S(2)}, u32[]{:S(2)}) async-start(bf16[8,32,512]{2,1,0:T(8,128)(2,1)} %bitcast.81), calls=%async_computation | async-start | bytes 524288 | tf_op jit(solution)/shard_map/all_to_all | solution.py:107
  14.6 0.7 compare_and_fusion.1
  15.3 1.0 sort.17
  16.3 0.8 reduce-window.18
  17.4 6.2 %all-to-all-done = bf16[8,32,512]{2,1,0:T(8,128)(2,1)S(1)} async-done(((bf16[8,32,512]{2,1,0:T(8,128)(2,1)}), bf16[8,32,512]{2,1,0:T(8,128)(2,1)S(1)}, u32[]{:S(2)}, u32[]{:S(2)}) %all-to-all-start) | async-done | bytes 262176 | tf_op jit(solution)/shard_map/all_to_all | solution.py:107
  23.5 0.6 gather_fusion
  24.1 0.1 bitcast_select_fusion
  24.3 0.6 fusion.53
  25.5 0.7 broadcast_compare_fusion
  26.2 0.6 slice.199
  26.8 0.1 maximum_select_fusion.1
  26.9 1.6 %collective-permute-start.1 = (bf16[256,1024]{1,0:T(8,128)(2,1)S(1)}, bf16[256,1024]{1,0:T(8,128)(2,1)S(1)}, u32[]{:S(2)}, u32[]{:S(2)}) collective-permute-start(bf16[256,1024]{1,0:T(8,128)(2,1)S(1)} %maximum_select_fusion.1), channel_id=1, source_target_pairs={{0,2},{1,3},{2,0},{3,1},{4,6},{5,7},{6,4},{7,5},{8,10},{9,11},{10,... | collective-permute-start | bytes 1572872 | tf_op jit(solution)/shard_map/ppermute | solution.py:120
  28.6 15.4 %collective-permute-done.1 = bf16[256,1024]{1,0:T(8,128)(2,1)S(1)} collective-permute-done((bf16[256,1024]{1,0:T(8,128)(2,1)S(1)}, bf16[256,1024]{1,0:T(8,128)(2,1)S(1)}, u32[]{:S(2)}, u32[]{:S(2)}) %collective-permute-start.1) | collective-permute-done | bytes 524320 | tf_op jit(solution)/shard_map/ppermute | solution.py:120
  44.0 0.4 fusion.41
  44.4 1.8 %reduce-window.19 = f32[6,2,128]{2,1,0:T(2,128)S(1)} reduce-window(f32[6,2,128]{2,1,0:T(2,128)S(1)} %reshape.288, f32[]{:T(128)} %constant.154.clone.1), window={size=1x1x128 pad=0_0x0_0x127_0}, to_apply=%region_3.4 | reduce-window | flops 195072 | bytes 12292 | tf_op jit(solution)/shard_map/reduce-window.1
  46.3 0.1 copy.40
  46.6 0.2 slice_reduce_fusion
  46.9 0.7 convolution_convert_fusion.2
  47.7 2.4 %convolution_convert_fusion = bf16[256,512]{1,0:T(8,128)(2,1)S(1)} fusion(bf16[2048,512]{1,0:T(8,128)(2,1)} %all-gather.2.cloned.1.call-done, bf16[256,1024]{1,0:T(8,128)(2,1)S(1)} %collective-permute-done.1, bf16[256,1024]{1,0:T(8,128)(2,1)S(1)} %maximum_select_fusion.1, pred[]{:T(512)S(6)} %eq.48), kind=kOutput, calls=%fused_computation.8 | convolution fusion | flops 541720576 | bytes 3407873 | tf_op jit(solution)/shard_map/dot_general | solution.py:127
  50.1 3.4 %collective-permute-start.2 = (bf16[3,896]{1,0:T(4,128)(2,1)S(1)}, bf16[3,896]{1,0:T(4,128)(2,1)S(1)}, u32[]{:S(2)}, u32[]{:S(2)}) collective-permute-start(bf16[3,896]{1,0:T(4,128)(2,1)S(1)} %pad_maximum_fusion.3), channel_id=1, source_target_pairs={{0,4},{4,8},{8,12},{12,16},{16,20},{20,24},{24,28},{1,5},{5,9},{9,... | collective-permute-start | bytes 16136 | tf_op jit(solution)/shard_map/ppermute | solution.py:12
  53.4 0.7 broadcast_select_fusion.1
  54.1 0.7 collective-permute-done.2
  54.9 0.7 divide_multiply_fusion
  55.6 0.2 copy.39
  55.8 0.5 fusion.25
  56.4 0.8 pad_maximum_fusion
  57.2 5.9 %collective-permute-start.4 = (f32[6,65,256]{2,1,0:T(8,128)}, f32[6,65,256]{2,1,0:T(8,128)}, u32[]{:S(2)}, u32[]{:S(2)}) collective-permute-start(f32[6,65,256]{2,1,0:T(8,128)} %pad_maximum_fusion), channel_id=1, source_target_pairs={{0,8},{4,12},{8,16},{12,20},{16,24},{20,28},{1,9},{5,13},{9,17},{1... | collective-permute-start | bytes 1198088 | tf_op jit(solution)/shard_map/ppermute | solution.py:12
  63.1 3.2 %collective-permute-start.3 = (f32[6,65,256]{2,1,0:T(8,128)}, f32[6,65,256]{2,1,0:T(8,128)}, u32[]{:S(2)}, u32[]{:S(2)}) collective-permute-start(f32[6,65,256]{2,1,0:T(8,128)} %pad_maximum_fusion), channel_id=1, source_target_pairs={{0,4},{4,8},{8,12},{12,16},{16,20},{20,24},{24,28},{1,5},{5,9},{9,... | collective-permute-start | bytes 1198088 | tf_op jit(solution)/shard_map/ppermute | solution.py:12
  66.4 0.8 fusion.49
  67.2 0.1 fusion.31
  67.3 3.7 %collective-permute-done.4 = f32[6,65,256]{2,1,0:T(8,128)} collective-permute-done((f32[6,65,256]{2,1,0:T(8,128)}, f32[6,65,256]{2,1,0:T(8,128)}, u32[]{:S(2)}, u32[]{:S(2)}) %collective-permute-start.4) | collective-permute-done | bytes 399392 | tf_op jit(solution)/shard_map/ppermute | solution.py:12
  71.0 3.0 %collective-permute-done.3 = f32[6,65,256]{2,1,0:T(8,128)} collective-permute-done((f32[6,65,256]{2,1,0:T(8,128)}, f32[6,65,256]{2,1,0:T(8,128)}, u32[]{:S(2)}, u32[]{:S(2)}) %collective-permute-start.3) | collective-permute-done | bytes 399392 | tf_op jit(solution)/shard_map/ppermute | solution.py:12
  73.9 0.8 fusion.47
  74.8 1.2 slice_add_fusion
  76.0 10.9 %collective-permute-start.5 = (f32[6,65,256]{2,1,0:T(8,128)S(1)}, f32[6,65,256]{2,1,0:T(8,128)S(1)}, u32[]{:S(2)}, u32[]{:S(2)}) collective-permute-start(f32[6,65,256]{2,1,0:T(8,128)S(1)} %pad_maximum_fusion.1), channel_id=1, source_target_pairs={{0,8},{4,12},{8,16},{12,20},{16,24},{20,28},{1,9},{5,13},{9,17},{1... | collective-permute-start | bytes 1198088 | tf_op jit(solution)/shard_map/ppermute | solution.py:12
  87.0 1.5 %fusion.10 = f32[256,384]{1,0:T(8,128)} fusion(bf16[2048,384]{1,0:T(8,128)(2,1)S(1)} %copy-done.6, bf16[256,1024]{1,0:T(8,128)(2,1)S(1)} %copy-done.8, bf16[256,1024]{1,0:T(8,128)(2,1)S(1)} %copy-done.2, pred[]{:T(512)S(6)} %eq.48), kind=kOutput, calls=%fused_computation.13 | convolution fusion | flops 407568384 | bytes 3014657 | tf_op jit(solution)/shard_map/dot_general | solution.py:127
  88.5 5.9 %collective-permute-done.5 = f32[6,65,256]{2,1,0:T(8,128)S(1)} collective-permute-done((f32[6,65,256]{2,1,0:T(8,128)S(1)}, f32[6,65,256]{2,1,0:T(8,128)S(1)}, u32[]{:S(2)}, u32[]{:S(2)}) %collective-permute-start.5) | collective-permute-done | bytes 399392 | tf_op jit(solution)/shard_map/ppermute | solution.py:12
  94.5 5.3 %collective-permute-start.6 = (f32[6,65,256]{2,1,0:T(8,128)S(1)}, f32[6,65,256]{2,1,0:T(8,128)S(1)}, u32[]{:S(2)}, u32[]{:S(2)}) collective-permute-start(f32[6,65,256]{2,1,0:T(8,128)S(1)} %pad_maximum_fusion.2), channel_id=1, source_target_pairs={{0,16},{4,20},{8,24},{12,28},{1,17},{5,21},{9,25},{13,29},{2,18},{... | collective-permute-start | bytes 1198088 | tf_op jit(solution)/shard_map/ppermute | solution.py:12
  99.8 0.4 fusion.33
  100.3 1.9 %fusion.5 = f32[256,6,64]{0,2,1:T(8,128)S(1)} fusion(f32[6,256]{1,0:T(8,128)S(1)} %bitcast.86, f32[256,256]{1,0:T(8,128)S(1)} %fusion.33, pred[256,256]{1,0:T(8,128)(4,1)S(1)} %fusion.31, f32[256,6,64]{0,2,1:T(8,128)S(1)} %bitcast.76, f32[256,6]{0,1:T(8,128)S(1)} %get-tuple-element.76), kind=kOutput, calls=%fused_computation.7 | convolution fusion | flops 303267840 | bytes 1126400 | tf_op jit(solution)/shard_map/hts,shp->thp/dot_general | solution.py:75
  102.1 4.3 %collective-permute-done.6 = f32[6,65,256]{2,1,0:T(8,128)S(1)} collective-permute-done((f32[6,65,256]{2,1,0:T(8,128)S(1)}, f32[6,65,256]{2,1,0:T(8,128)S(1)}, u32[]{:S(2)}, u32[]{:S(2)}) %collective-permute-start.6) | collective-permute-done | bytes 399392 | tf_op jit(solution)/shard_map/ppermute | solution.py:12
  106.4 0.5 fusion.9
  106.9 0.2 copy.42
  107.1 1.1 multiply_convert_fusion
  108.2 0.6 gather_fusion.1
  108.9 22.9 %all_to_all.10 = bf16[8,32,384]{2,1,0:T(8,128)(2,1)S(1)} all-to-all(bf16[8,32,384]{2,1,0:T(8,128)(2,1)S(1)} %broadcast_select_fusion), channel_id=1, replica_groups=mesh['seq'=8,'fsdp'=4] {'seq'}, dimensions={0} | all-to-all | bytes 393216 | tf_op jit(solution)/shard_map/all_to_all | solution.py:166
  131.9 0.7 copy.63
  (62 shorter events, 1.4 us)
Async XLA Ops:
  6.5 40.4 %copy-start = (bf16[2048,384]{1,0:T(8,128)(2,1)S(1)}, bf16[2048,384]{1,0:T(8,128)(2,1)}, u32[]{:S(2)}) copy-start(bf16[2048,384]{1,0:T(8,128)(2,1)} %param.23) | copy-start | bytes 4718596
  6.5 22.0 %copy-start.4 = (f32[4,384]{1,0:T(4,128)S(1)}, f32[4,384]{1,0:T(4,128)}, u32[]{:S(2)}) copy-start(f32[4,384]{1,0:T(4,128)} %param.27) | copy-start | bytes 18436
  6.5 22.0 %copy-start.3 = (f32[4,512]{1,0:T(4,128)S(1)}, f32[4,512]{1,0:T(4,128)}, u32[]{:S(2)}) copy-start(f32[4,512]{1,0:T(4,128)} %param.28) | copy-start | bytes 24580
  6.5 22.0 %copy-start.10 = (f32[6]{0:T(128)S(1)}, f32[6]{0:T(128)}, u32[]{:S(2)}) copy-start(f32[6]{0:T(128)} %param.30) | copy-start | bytes 76
  6.5 37.4 %copy-start.11 = (f32[6]{0:T(128)S(1)}, f32[6]{0:T(128)}, u32[]{:S(2)}) copy-start(f32[6]{0:T(128)} %param.29) | copy-start | bytes 76
  6.5 37.4 %copy-start.9 = (bf16[2048,6]{0,1:T(8,128)(2,1)S(1)}, bf16[2048,6]{0,1:T(8,128)(2,1)}, u32[]{:S(2)}) copy-start(bf16[2048,6]{0,1:T(8,128)(2,1)} %param.26) | copy-start | bytes 73732
  6.6 41.1 %all-gather.2.cloned.1.call-start = ((), (), s32[]{:S(2)}) async-start(), calls=%async_computation.2 | async-start | bytes 2621440 | tf_op jit(solution)/shard_map/all_gather | solution.py:115
  7.3 16.2 %all-to-all-start = ((bf16[8,32,512]{2,1,0:T(8,128)(2,1)}), bf16[8,32,512]{2,1,0:T(8,128)(2,1)S(1)}, u32[]{:S(2)}, u32[]{:S(2)}) async-start(bf16[8,32,512]{2,1,0:T(8,128)(2,1)} %bitcast.81), calls=%async_computation | async-start | bytes 524288 | tf_op jit(solution)/shard_map/all_to_all | solution.py:107
  24.2 2.6 %collective-permute-start = (bf16[256,512]{1,0:T(8,128)(2,1)S(1)}, bf16[256,512]{1,0:T(8,128)(2,1)S(1)}, u32[]{:S(2)}, u32[]{:S(2)}) collective-permute-start(bf16[256,512]{1,0:T(8,128)(2,1)S(1)} %bitcast_select_fusion), channel_id=1, source_target_pairs={{0,1},{1,0},{2,3},{3,2},{4,5},{5,4},{6,7},{7,6},{8,9},{9,8},{10,11... | collective-permute-start | bytes 786440 | tf_op jit(solution)/shard_map/ppermute | solution.py:120
  26.9 20.7 %copy-start.1 = (bf16[256,1024]{1,0:T(8,128)(2,1)}, bf16[256,1024]{1,0:T(8,128)(2,1)S(1)}, u32[]{:S(2)}) copy-start(bf16[256,1024]{1,0:T(8,128)(2,1)S(1)} %maximum_select_fusion.1) | copy-start | bytes 1572868
  26.9 17.0 %collective-permute-start.1 = (bf16[256,1024]{1,0:T(8,128)(2,1)S(1)}, bf16[256,1024]{1,0:T(8,128)(2,1)S(1)}, u32[]{:S(2)}, u32[]{:S(2)}) collective-permute-start(bf16[256,1024]{1,0:T(8,128)(2,1)S(1)} %maximum_select_fusion.1), channel_id=1, source_target_pairs={{0,2},{1,3},{2,0},{3,1},{4,6},{5,7},{6,4},{7,5},{8,10},{9,11},{10,... | collective-permute-start | bytes 1572872 | tf_op jit(solution)/shard_map/ppermute | solution.py:120
  44.0 3.7 %copy-start.7 = (bf16[256,1024]{1,0:T(8,128)(2,1)}, bf16[256,1024]{1,0:T(8,128)(2,1)S(1)}, u32[]{:S(2)}) copy-start(bf16[256,1024]{1,0:T(8,128)(2,1)S(1)} %collective-permute-done.1) | copy-start | bytes 1572868
  50.1 4.7 %collective-permute-start.2 = (bf16[3,896]{1,0:T(4,128)(2,1)S(1)}, bf16[3,896]{1,0:T(4,128)(2,1)S(1)}, u32[]{:S(2)}, u32[]{:S(2)}) collective-permute-start(bf16[3,896]{1,0:T(4,128)(2,1)S(1)} %pad_maximum_fusion.3), channel_id=1, source_target_pairs={{0,4},{4,8},{8,12},{12,16},{16,20},{20,24},{24,28},{1,5},{5,9},{9,... | collective-permute-start | bytes 16136 | tf_op jit(solution)/shard_map/ppermute | solution.py:12
  55.8 31.2 %copy-start.2 = (bf16[256,1024]{1,0:T(8,128)(2,1)S(1)}, bf16[256,1024]{1,0:T(8,128)(2,1)}, u32[]{:S(2)}) copy-start(bf16[256,1024]{1,0:T(8,128)(2,1)} %copy-done.1) | copy-start | bytes 1572868
  57.2 13.8 %collective-permute-start.4 = (f32[6,65,256]{2,1,0:T(8,128)}, f32[6,65,256]{2,1,0:T(8,128)}, u32[]{:S(2)}, u32[]{:S(2)}) collective-permute-start(f32[6,65,256]{2,1,0:T(8,128)} %pad_maximum_fusion), channel_id=1, source_target_pairs={{0,8},{4,12},{8,16},{12,20},{16,24},{20,28},{1,9},{5,13},{9,17},{1... | collective-permute-start | bytes 1198088 | tf_op jit(solution)/shard_map/ppermute | solution.py:12
  63.1 10.9 %collective-permute-start.3 = (f32[6,65,256]{2,1,0:T(8,128)}, f32[6,65,256]{2,1,0:T(8,128)}, u32[]{:S(2)}, u32[]{:S(2)}) collective-permute-start(f32[6,65,256]{2,1,0:T(8,128)} %pad_maximum_fusion), channel_id=1, source_target_pairs={{0,4},{4,8},{8,12},{12,16},{16,20},{20,24},{24,28},{1,5},{5,9},{9,... | collective-permute-start | bytes 1198088 | tf_op jit(solution)/shard_map/ppermute | solution.py:12
  66.4 20.6 %copy-start.6 = (bf16[2048,384]{1,0:T(8,128)(2,1)S(1)}, bf16[2048,384]{1,0:T(8,128)(2,1)}, u32[]{:S(2)}) copy-start(bf16[2048,384]{1,0:T(8,128)(2,1)} %param.24) | copy-start | bytes 4718596
  66.4 20.6 %copy-start.8 = (bf16[256,1024]{1,0:T(8,128)(2,1)S(1)}, bf16[256,1024]{1,0:T(8,128)(2,1)}, u32[]{:S(2)}) copy-start(bf16[256,1024]{1,0:T(8,128)(2,1)} %copy-done.7) | copy-start | bytes 1572868
  76.0 18.4 %collective-permute-start.5 = (f32[6,65,256]{2,1,0:T(8,128)S(1)}, f32[6,65,256]{2,1,0:T(8,128)S(1)}, u32[]{:S(2)}, u32[]{:S(2)}) collective-permute-start(f32[6,65,256]{2,1,0:T(8,128)S(1)} %pad_maximum_fusion.1), channel_id=1, source_target_pairs={{0,8},{4,12},{8,16},{12,20},{16,24},{20,28},{1,9},{5,13},{9,17},{1... | collective-permute-start | bytes 1198088 | tf_op jit(solution)/shard_map/ppermute | solution.py:12
  94.5 11.9 %copy-start.5 = (f32[6]{0:T(128)S(1)}, f32[6]{0:T(128)}, u32[]{:S(2)}) copy-start(f32[6]{0:T(128)} %param.31) | copy-start | bytes 76
  94.5 11.9 %collective-permute-start.6 = (f32[6,65,256]{2,1,0:T(8,128)S(1)}, f32[6,65,256]{2,1,0:T(8,128)S(1)}, u32[]{:S(2)}, u32[]{:S(2)}) collective-permute-start(f32[6,65,256]{2,1,0:T(8,128)S(1)} %pad_maximum_fusion.2), channel_id=1, source_target_pairs={{0,16},{4,20},{8,24},{12,28},{1,17},{5,21},{9,25},{13,29},{2,18},{... | collective-permute-start | bytes 1198088 | tf_op jit(solution)/shard_map/ppermute | solution.py:12
Sparse Core Ops, SparseCore 0:
  9.0 28.0 all-gather.1
